TPU v7x, 32 devices: a whole 2x2x4 slice. The times are simulated.
32 devices in a mesh: groups: 2 (over y), picks: 4 (over z), heads: 4 (over x, core).
Axes of the slice: x: 2, y: 2, z: 4, core: 2. Of those that a mesh axis runs over, the one named last changes fastest.
Arguments:
- coords: float32 [3, 8192], P(None, ('groups', 'picks')), parts along dimension 1, may hold values from -1 to 1
- horizon_ids: int32 [8192], P(('groups', 'picks')), parts along dimension 0, may hold values from 0 to 63
- horizon_levels: float32 [128], P('groups'), parts along dimension 0, may hold values from -2 to 2
- latents: bfloat16 [512, 1024], replicated, may hold values from -960 to 960
- kv_weight: bfloat16 [3072, 2, 1024], P('picks', None, 'heads'), may hold values from -0.109375 to 0.109375
- cross_out: bfloat16 [1024, 1024], P('heads'), may hold values from -0.75 to 0.75
- norm_gains: float32 [2, 1024], replicated, may hold values from 0.1 to 1.9
- self_qkv: bfloat16 [3, 1024, 1024], P(None, None, 'heads'), may hold values from -0.1875 to 0.1875
- self_out: bfloat16 [1024, 1024], P(None, 'heads'), may hold values from -0.1875 to 0.1875
- dec_kv: bfloat16 [2, 1024, 1024], P(None, None, 'heads'), may hold values from -0.1875 to 0.1875
- dec_query: bfloat16 [3072, 1024], P('picks', 'heads'), may hold values from -0.109375 to 0.109375
- readout: float32 [1024], P('heads'), may hold values from -0.1875 to 0.1875
Outputs:
- field: float32 [8192], P(('groups', 'picks')), parts along dimension 0
- latents_out: float32 [1024, 1024], P('groups', 'heads'), parts along dimension 0
- grad_query: float32 [6144, 1024], P(('groups', 'picks'), 'heads'), parts along dimension 0
There are 2 independent parts, one for each index of `groups`. A program takes and returns all parts, laid end to end along the dimension named above; an argument that names none is the same for every part. Nothing has to cross between parts.
All inputs are finite; a program needn't handle non-finite values.
Results may differ from a plain program's by a relative error of at most 0.028.
Values may be sent and summed in bfloat16 or wider, within the bound.
No kernel may reach another device: no remote copies, remote signals or barrier semaphores. Data moves between devices by JAX's collectives and lax.ppermute only.
A program may use at most 64 MiB of HBM per device.

v0:
```python
import functools
import jax
import jax.numpy as jnp
from jax import lax
from jax.sharding import PartitionSpec as P

HEAD = 128
BANDS = 512
HORIZONS = 64
PI = 3.141592653589793
EPS = 1e-06
RING_MAX = 4


def encode(coords):
    freq = jnp.linspace(1.0, BANDS / 2.0, BANDS).astype(jnp.float32)
    angle = PI * freq[None, :, None] * coords[:, None, :]
    table = jnp.concatenate([jnp.sin(angle), jnp.cos(angle)], axis=0)
    return table.reshape(6 * BANDS, coords.shape[1]).T.astype(jnp.bfloat16)


def ring_gather(x, axis, n):
    if n == 1:
        return x
    if n > RING_MAX:
        return lax.all_gather(x, axis, axis=0, tiled=True)
    idx = lax.axis_index(axis)
    blocks = [x]
    for s in range(1, n):
        blocks.append(lax.ppermute(x, axis, [(i, (i - s) % n) for i in range(n)]))
    flipped = jnp.stack(blocks)
    ordered = jnp.roll(flipped, idx, axis=0)
    return ordered.reshape((n * x.shape[0],) + x.shape[1:])


def on_device(
    coords,
    horizon_ids,
    horizon_levels,
    latents,
    kv_weight,
    cross_out,
    norm_gains,
    self_qkv,
    self_out,
    dec_kv,
    dec_query,
    readout,
    *,
    n_picks,
    n_heads
):
    high = lax.Precision.HIGHEST
    scale = HEAD ** (-0.5)
    count = coords.shape[1]
    width = latents.shape[1]
    lat_rows = latents.shape[0]
    local = kv_weight.shape[2]
    nheads = local // HEAD
    column = lax.axis_index("heads") * local
    enc = encode(coords)
    cross_full = ring_gather(cross_out, "heads", n_heads)
    piece = lax.all_gather(kv_weight, "picks", axis=0, tiled=True)
    keys_vals = jnp.dot(
        enc, piece.reshape(piece.shape[0], 2 * local), preferred_element_type=jnp.float32
    ).astype(jnp.bfloat16)
    keys = keys_vals[:, :local].reshape(count, nheads, HEAD)
    values = keys_vals[:, local:].reshape(count, nheads, HEAD)
    queries = lax.dynamic_slice_in_dim(latents, column, local, 1).reshape(lat_rows, nheads, HEAD)
    scores = jnp.einsum("lhc,thc->hlt", queries, keys, preferred_element_type=jnp.float32) * scale
    top = jnp.max(scores, axis=2)
    expo = jnp.exp(scores - top[:, :, None])
    total = jnp.sum(expo, axis=2)
    numer = jnp.einsum(
        "hlt,thc->hlc", expo.astype(jnp.bfloat16), values, preferred_element_type=jnp.float32
    )
    all_numer = lax.all_gather(numer.astype(jnp.bfloat16), "picks", axis=0, tiled=False)
    all_stats = lax.all_gather(jnp.stack([top, total]), "picks", axis=0, tiled=False)
    best = jnp.max(all_stats[:, 0], axis=0)
    factor = jnp.exp(all_stats[:, 0] - best[None])
    merged_total = jnp.sum(factor * all_stats[:, 1], axis=0)
    merged_numer = jnp.einsum(
        "phl,phlc->hlc", factor, all_numer.astype(jnp.float32), precision=high
    )
    attended = (
        (merged_numer / merged_total[:, :, None])
        .transpose(1, 0, 2)
        .reshape(lat_rows, local)
        .astype(jnp.bfloat16)
    )
    dq_local, attended = lax.optimization_barrier((dec_query, attended))
    dq_full = ring_gather(dq_local, "picks", n_picks)
    gain_two = lax.dynamic_slice_in_dim(norm_gains[1], column, local, 0)
    attended_full = lax.all_gather(attended, "heads", axis=1, tiled=True)
    whole = latents.astype(jnp.float32) + jnp.dot(
        attended_full, cross_full, preferred_element_type=jnp.float32
    )
    power = jnp.mean(whole * whole, axis=1, keepdims=True)
    normed = (whole * lax.rsqrt(power + EPS) * norm_gains[0][None, :]).astype(jnp.bfloat16)
    state = lax.dynamic_slice_in_dim(whole, column, local, 1)
    qkv = jnp.einsum("ld,kde->kle", normed, self_qkv, preferred_element_type=jnp.float32).astype(
        jnp.bfloat16
    )
    self_q = qkv[0].reshape(lat_rows, nheads, HEAD)
    self_k = qkv[1].reshape(lat_rows, nheads, HEAD)
    self_v = qkv[2].reshape(lat_rows, nheads, HEAD)
    inner = jnp.einsum("lhc,mhc->hlm", self_q, self_k, preferred_element_type=jnp.float32) * scale
    raised = jnp.exp(inner)
    probs = (raised / jnp.sum(raised, axis=2, keepdims=True)).astype(jnp.bfloat16)
    head_out = (
        jnp.einsum("hlm,mhc->lhc", probs, self_v, preferred_element_type=jnp.float32)
        .astype(jnp.bfloat16)
        .reshape(lat_rows, local)
    )
    every_head = lax.all_gather(head_out, "heads", axis=1, tiled=True)
    latents_out = state + jnp.dot(every_head, self_out, preferred_element_type=jnp.float32)
    gained = (latents_out * gain_two[None, :]).astype(jnp.bfloat16)
    gained_full = lax.all_gather(gained, "heads", axis=1, tiled=True)
    power_two = lax.psum(jnp.sum(latents_out * latents_out, axis=1), "heads")
    row_scale = lax.rsqrt(power_two / width + EPS)
    dec = (
        jnp.einsum("ld,kde->kle", gained_full, dec_kv, preferred_element_type=jnp.float32)
        * row_scale[None, :, None]
    ).astype(jnp.bfloat16)
    dec_keys = dec[0].reshape(lat_rows, nheads, HEAD)
    dec_vals = dec[1].reshape(lat_rows, nheads, HEAD)
    query = jnp.dot(enc, dq_full, preferred_element_type=jnp.float32).astype(jnp.bfloat16)
    dec_q = query.reshape(count, nheads, HEAD)
    logits = jnp.einsum("thc,lhc->htl", dec_q, dec_keys, preferred_element_type=jnp.float32) * scale
    lifted = jnp.exp(logits)
    weights = lifted / jnp.sum(lifted, axis=2, keepdims=True)
    out = jnp.einsum(
        "htl,lhc->thc", weights.astype(jnp.bfloat16), dec_vals, preferred_element_type=jnp.float32
    )
    read = readout.reshape(nheads, HEAD)
    field = lax.psum(jnp.sum(out * read[None, :, :], axis=(1, 2)), "heads")
    onehot = (horizon_ids[:, None] == jnp.arange(HORIZONS, dtype=jnp.int32)[None, :]).astype(
        jnp.float32
    )
    target = jnp.sum(onehot * horizon_levels[None, :], axis=1)
    miss = field - target
    value_read = jnp.einsum("lhc,hc->hl", dec_vals.astype(jnp.float32), read, precision=high)
    dprob = miss[None, :, None] * value_read[:, None, :]
    dscore = (weights * (dprob - jnp.sum(dprob * weights, axis=2, keepdims=True))).astype(
        jnp.bfloat16
    )
    dquery = (
        (jnp.einsum("htl,lhc->thc", dscore, dec_keys, preferred_element_type=jnp.float32) * scale)
        .reshape(count, local)
        .astype(jnp.bfloat16)
    )
    grad_query = lax.psum_scatter(
        jnp.dot(enc.T, dquery, preferred_element_type=jnp.float32).astype(jnp.bfloat16),
        "picks",
        scatter_dimension=0,
        tiled=True,
    ).astype(jnp.float32)
    return (field, latents_out, grad_query)


def solution(mesh):
    in_specs = (
        P(None, ("groups", "picks")),
        P(("groups", "picks")),
        P("groups"),
        P(),
        P("picks", None, "heads"),
        P("heads", None),
        P(),
        P(None, None, "heads"),
        P(None, "heads"),
        P(None, None, "heads"),
        P("picks", "heads"),
        P("heads"),
    )
    out_specs = (P(("groups", "picks")), P("groups", "heads"), P(("groups", "picks"), "heads"))
    body = functools.partial(on_device, n_picks=mesh.shape["picks"], n_heads=mesh.shape["heads"])
    return jax.shard_map(body, mesh=mesh, in_specs=in_specs, out_specs=out_specs, check_vma=False)
```

profile of v0, /device:TPU:0, one launch (start us, length us, event | category | flops | bytes accessed | tf_op | source)
XLA Modules:
  0.0 272.0 jit_solution(7602422129302060528)
XLA Ops:
  8.0 1.0 constant_dynamic-slice_fusion.3
  9.2 23.6 %fusion = (bf16[3,512,1024]{2,1,0:T(8,128)(2,1)S(1)}, bf16[3,512,1024]{2,1,0:T(8,128)(2,1)S(1)}) fusion(f32[3,1024]{1,0:T(4,128)} %param.12, f32[512]{0:T(512)S(1)} %maximum_multiply_fusion), kind=kLoop, calls=%fused_computation.2 | loop fusion | flops 4718592 | bytes 6305792 | tf_op jit(solution)/shard_map/convert
  32.8 3.2 %pad_maximum_fusion = bf16[6,512,1024]{2,1,0:T(8,128)(2,1)} fusion(bf16[3,512,1024]{2,1,0:T(8,128)(2,1)S(1)} %get-tuple-element.19, bf16[3,512,1024]{2,1,0:T(8,128)(2,1)S(1)} %get-tuple-element.18), kind=kLoop, calls=%fused_computation.4 | loop fusion | flops 3145728 | bytes 12582912 | tf_op jit(solution)/shard_map/concatenate | solution.py:18
  36.0 39.9 %all-gather.8.cloned.1.call-done = bf16[3072,2,256]{2,1,0:T(2,128)(2,1)} async-done(((bf16[768,2,256]{2,1,0:T(2,128)(2,1)}), bf16[3072,2,256]{2,1,0:T(2,128)(2,1)}) %all-gather.8.cloned.1.call-update) | async-done | bytes 3145744 | tf_op jit(solution)/shard_map/all_gather | solution.py:63
  75.8 2.6 copy.98
  78.4 1.1 copy-done.5
  79.6 3.5 %convolution_convert_fusion.1 = bf16[1024,512]{0,1:T(8,128)(2,1)S(1)} fusion(bf16[3072,1024]{1,0:T(8,128)(2,1)S(1)} %bitcast.122, bf16[3072,512]{1,0:T(8,128)(2,1)S(1)} %bitcast.127), kind=kOutput, calls=%fused_computation.33 | convolution fusion | flops 3221749760 | bytes 10485760 | tf_op jit(solution)/shard_map/dot_general | solution.py:64
  83.2 0.8 multiply_reduce_fusion
  84.1 2.0 copy-done.2
  86.1 1.6 fusion.36
  87.8 0.9 collective-permute-start
  89.5 0.8 bitcast_dynamic-update-slice_fusion.6
  90.4 10.5 %collective-permute-done = bf16[256,1024]{1,0:T(8,128)(2,1)S(1)} collective-permute-done((bf16[256,1024]{1,0:T(8,128)(2,1)S(1)}, bf16[256,1024]{1,0:T(8,128)(2,1)S(1)}, u32[]{:S(2)}, u32[]{:S(2)}) %collective-permute-start) | collective-permute-done | bytes 524320 | tf_op jit(solution)/shard_map/ppermute | solution.py:30
  100.8 0.8 bitcast_dynamic-update-slice_fusion.4
  101.7 3.1 %fusion.7 = f32[2,512]{1,0:T(2,128)S(1)} fusion(f32[2,512,1024]{2,1,0:T(8,128)} %copy-done.2, f32[2,512]{1,0:T(2,128)S(1)} %get-tuple-element.22), kind=kLoop, calls=%fused_computation.16 | loop fusion | flops 3144704 | bytes 4202496 | tf_op jit(solution)/shard_map/reduce_sum | solution.py:73
  104.8 13.3 %all-gather.1 = f32[8,2,512]{2,1,0:T(2,128)S(1)} all-gather(f32[2,2,512]{2,1,0:T(2,128)S(1)} %pad_maximum_fusion.1), channel_id=3, replica_groups=mesh['groups'=2,'picks'=4,'heads'=4] {'picks'}, dimensions={0}, use_global_device_ids=true | all-gather | bytes 40960 | tf_op jit(solution)/shard_map/all_gather | solution.py:78
  118.1 1.0 copy.81
  119.3 5.3 %fusion.44 = f32[512,2,1,128]{3,2,1,0:T(1,128)S(1)} fusion(f32[4,2,512,1]{0,3,1,2:T(1,128)} %copy.81, bf16[4,2,512,128]{3,2,1,0:T(8,128)(2,1)} %bitcast.156), kind=kOutput, calls=%fused_computation.51 | convolution fusion | flops 6291456 | bytes 1589248 | tf_op jit(solution)/shard_map/phl,phlc->hlc/dot_general | solution.py:82
  126.2 0.8 bitcast_dynamic-update-slice_fusion.2
  127.0 1.9 bitcast_dynamic-update-slice_fusion
  128.9 0.9 bitcast_dynamic-update-slice_fusion.7
  129.8 0.8 bitcast_dynamic-update-slice_fusion.5
  130.6 0.9 bitcast_dynamic-update-slice_fusion.3
  131.5 1.9 bitcast_dynamic-update-slice_fusion.1
  133.3 3.1 %constant_dynamic-slice_fusion.2 = bf16[4,256,1024]{2,1,0:T(8,128)(2,1)} fusion(bf16[8,256,1024]{2,1,0:T(8,128)(2,1)} %bitcast_dynamic-update-slice_fusion.1, s32[]{:T(128)S(6)} %select_n.30), kind=kLoop, calls=%fused_computation.93 | loop fusion | bytes 4194308 | tf_op jit(solution)/shard_map/jit(_roll_dynamic)/dynamic_slice | solution.py:32
  136.4 4.8 %all-gather.10.cloned.1.call-done = bf16[512,1024]{1,0:T(8,128)(2,1)} async-done(((bf16[512,256]{1,0:T(8,128)(2,1)}), bf16[512,1024]{1,0:T(8,128)(2,1)}) %all-gather.10.cloned.1.call-update) | async-done | bytes 1048592 | tf_op jit(solution)/shard_map/all_gather | solution.py:94
  141.2 3.5 %multiply_reduce_fusion.1 = (f32[512]{0:T(512)S(1)}, f32[512,1024]{1,0:T(8,128)S(1)}) fusion(bf16[512,1024]{1,0:T(8,128)(2,1)} %all-gather.10.cloned.1.call-done, bf16[1024,1024]{1,0:T(8,128)(2,1)} %bitcast.128, bf16[512,1024]{1,0:T(8,128)(2,1)} %param.15), kind=kOutput, calls=%fused_computation.28 | convolution fusion | flops 1075838464 | bytes 6293504 | tf_op jit(solution)/shard_map/dot_general | solution.py:95
  144.7 1.1 fusion.31
  146.5 1.2 convolution_convert_fusion.4
  147.8 3.4 %collective-permute-start.3 = (bf16[768,256]{1,0:T(8,128)(2,1)S(1)}, bf16[768,256]{1,0:T(8,128)(2,1)S(1)}, u32[]{:S(2)}, u32[]{:S(2)}) collective-permute-start(bf16[768,256]{1,0:T(8,128)(2,1)S(1)} %copy-done.7), channel_id=1, source_target_pairs={{0,12},{4,0},{8,4},{12,8},{1,13},{5,1},{9,5},{13,9},{2,14},{6,2},{... | collective-permute-start | bytes 1179656 | tf_op jit(solution)/shard_map/ppermute | solution.py:30
  151.4 1.1 collective-permute-start.5
  153.3 7.5 %collective-permute-done.3 = bf16[768,256]{1,0:T(8,128)(2,1)S(1)} collective-permute-done((bf16[768,256]{1,0:T(8,128)(2,1)S(1)}, bf16[768,256]{1,0:T(8,128)(2,1)S(1)}, u32[]{:S(2)}, u32[]{:S(2)}) %collective-permute-start.3) | collective-permute-done | bytes 393248 | tf_op jit(solution)/shard_map/ppermute | solution.py:30
  161.5 23.8 %collective-permute-done.4 = bf16[768,256]{1,0:T(8,128)(2,1)S(1)} collective-permute-done((bf16[768,256]{1,0:T(8,128)(2,1)S(1)}, bf16[768,256]{1,0:T(8,128)(2,1)S(1)}, u32[]{:S(2)}, u32[]{:S(2)}) %collective-permute-start.4) | collective-permute-done | bytes 393248 | tf_op jit(solution)/shard_map/ppermute | solution.py:30
  187.7 2.7 multiply_reduce_fusion.2
  190.5 0.8 bitcast_dynamic-update-slice_fusion.13
  193.0 1.5 constant_dynamic-slice_fusion
  194.5 5.0 %convolution_convert_fusion.3 = bf16[1024,256]{0,1:T(8,128)(2,1)S(1)} fusion(bf16[3072,1024]{1,0:T(8,128)(2,1)} %bitcast.121, bf16[3072,256]{1,0:T(8,128)(2,1)S(1)} %bitcast.130), kind=kOutput, calls=%fused_computation.39 | convolution fusion | flops 1610874880 | bytes 8388608 | tf_op jit(solution)/shard_map/dot_general | solution.py:127
  199.5 6.3 %psum.14 = f32[512]{0:T(512)S(1)} all-reduce(f32[512]{0:T(512)S(1)} %get-tuple-element.14), channel_id=1, replica_groups=mesh['groups'=2,'picks'=4,'heads'=4] {'heads'}, use_global_device_ids=true, to_apply=%region_7.8 | all-reduce | flops 512 | bytes 4096 | tf_op jit(solution)/shard_map/psum | solution.py:119
  206.3 2.0 fusion.35
  208.4 0.8 fusion.6
  209.2 2.0 copy-done.3
  211.2 1.0 fusion.32
  212.2 5.9 %psum.15 = f32[1024]{0:T(1024)S(1)} all-reduce(f32[1024]{0:T(1024)S(1)} %fusion.32), channel_id=1, replica_groups=mesh['groups'=2,'picks'=4,'heads'=4] {'heads'}, use_global_device_ids=true, to_apply=%region_10.11 | all-reduce | flops 1024 | bytes 8192 | tf_op jit(solution)/shard_map/psum | solution.py:136
  218.4 3.3 %fusion.2 = f32[2,1024]{1,0:T(2,128)S(1)} fusion(f32[2,512]{1,0:T(2,128)S(1)} %bitcast.149, f32[1024]{0:T(1024)S(1)} %sub.53, f32[2,1024]{1,0:T(2,128)S(1)} %get-tuple-element.29, f32[2,1024,512]{1,2,0:T(8,128)} %copy-done.3), kind=kLoop, calls=%fused_computation.7 | loop fusion | flops 5240832 | bytes 4218880 | tf_op jit(solution)/shard_map/reduce_sum | solution.py:144
  221.7 1.4 fusion.28
  223.7 3.1 %convolution_convert_fusion = bf16[3072,256]{1,0:T(8,128)(2,1)} fusion(bf16[3072,1024]{1,0:T(8,128)(2,1)S(1)} %bitcast.125, bf16[1024,256]{0,1:T(8,128)(2,1)S(1)} %bitcast.157), kind=kOutput, calls=%fused_computation.13 | convolution fusion | flops 1611399168 | bytes 8388608 | tf_op jit(solution)/shard_map/dot_general | solution.py:153
  226.8 36.4 %reduce-scatter.2.cloned.1.call-done = bf16[768,256]{1,0:T(8,128)(2,1)} async-done(((bf16[3072,256]{1,0:T(8,128)(2,1)}), bf16[768,256]{1,0:T(8,128)(2,1)}) %reduce-scatter.2.cloned.1.call-update) | async-done | bytes 393232 | tf_op jit(solution)/shard_map/reduce_scatter | solution.py:152
  263.2 1.9 convert_element_type.100
  (83 shorter events, 11.6 us)
Async XLA Ops:
  7.2 137.6 %copy-start = (bf16[3,1024,256]{2,1,0:T(8,128)(2,1)S(1)}, bf16[3,1024,256]{2,1,0:T(8,128)(2,1)}, u32[]{:S(2)}) copy-start(bf16[3,1024,256]{2,1,0:T(8,128)(2,1)} %param.19) | copy-start | bytes 4718596
  7.2 68.7 %all-gather.8.cloned.1.call-start = ((), (), s32[]{:S(2)}) async-start(), calls=%async_computation.1 | async-start | bytes 3932160 | tf_op jit(solution)/shard_map/all_gather | solution.py:63
  7.9 111.4 %all-gather.16.cloned.1.call-start = ((), (), s32[]{:S(2)}) async-start(), calls=%async_computation.6 | async-start | bytes 1310720 | tf_op jit(solution)/shard_map/all_gather | solution.py:77
  75.8 3.7 %copy-start.5 = (bf16[6,512,1024]{2,1,0:T(8,128)(2,1)S(1)}, bf16[6,512,1024]{2,1,0:T(8,128)(2,1)}, u32[]{:S(2)}) copy-start(bf16[6,512,1024]{2,1,0:T(8,128)(2,1)} %pad_maximum_fusion) | copy-start | bytes 18874372
  83.2 4.6 %copy-start.6 = (bf16[256,1024]{1,0:T(8,128)(2,1)S(1)}, bf16[256,1024]{1,0:T(8,128)(2,1)}, u32[]{:S(2)}) copy-start(bf16[256,1024]{1,0:T(8,128)(2,1)} %param.17) | copy-start | bytes 1572868
  83.2 6.3 %copy-start.9 = (f32[2,1024]{1,0:T(2,128)S(1)}, f32[2,1024]{1,0:T(2,128)}, u32[]{:S(2)}) copy-start(f32[2,1024]{1,0:T(2,128)} %param.18) | copy-start | bytes 24580
  84.1 2.0 copy-start.2
  87.7 53.5 %all-gather.10.cloned.1.call-start = ((), (), s32[]{:S(2)}) async-start(), calls=%async_computation.2 | async-start | bytes 1310720 | tf_op jit(solution)/shard_map/all_gather | solution.py:94
  87.8 13.1 %collective-permute-start = (bf16[256,1024]{1,0:T(8,128)(2,1)S(1)}, bf16[256,1024]{1,0:T(8,128)(2,1)S(1)}, u32[]{:S(2)}, u32[]{:S(2)}) collective-permute-start(bf16[256,1024]{1,0:T(8,128)(2,1)S(1)} %copy-done.6), channel_id=1, source_target_pairs={{0,3},{1,0},{2,1},{3,2},{4,7},{5,4},{6,5},{7,6},{8,11},{9,8},{10,9... | collective-permute-start | bytes 1572872 | tf_op jit(solution)/shard_map/ppermute | solution.py:30
  88.7 37.5 %collective-permute-start.1 = (bf16[256,1024]{1,0:T(8,128)(2,1)S(1)}, bf16[256,1024]{1,0:T(8,128)(2,1)S(1)}, u32[]{:S(2)}, u32[]{:S(2)}) collective-permute-start(bf16[256,1024]{1,0:T(8,128)(2,1)S(1)} %copy-done.6), channel_id=1, source_target_pairs={{0,2},{1,3},{2,0},{3,1},{4,6},{5,7},{6,4},{7,5},{8,10},{9,11},{10,... | collective-permute-start | bytes 1572872 | tf_op jit(solution)/shard_map/ppermute | solution.py:30
  89.4 37.7 %collective-permute-start.2 = (bf16[256,1024]{1,0:T(8,128)(2,1)S(1)}, bf16[256,1024]{1,0:T(8,128)(2,1)}, u32[]{:S(2)}, u32[]{:S(2)}) collective-permute-start(bf16[256,1024]{1,0:T(8,128)(2,1)S(1)} %copy-done.6), channel_id=1, source_target_pairs={{0,1},{1,2},{2,3},{3,0},{4,5},{5,6},{6,7},{7,4},{8,9},{9,10},{10,1... | collective-permute-start | bytes 1572872 | tf_op jit(solution)/shard_map/ppermute | solution.py:30
  126.1 61.6 %all-gather.12.cloned.1.call-start = ((), (), s32[]{:S(2)}) async-start(), calls=%async_computation.3 | async-start | bytes 1310720 | tf_op jit(solution)/shard_map/all_gather | solution.py:115
  144.7 1.8 copy-start.15
  146.5 1.4 copy-start.7
  146.5 4.7 %copy-start.10 = (s32[1024]{0:T(1024)S(1)}, s32[1024]{0:T(1024)}, u32[]{:S(2)}) copy-start(s32[1024]{0:T(1024)} %param.13) | copy-start | bytes 12292
  146.5 4.7 %copy-start.12 = (f32[64]{0:T(128)S(1)}, f32[64]{0:T(128)}, u32[]{:S(2)}) copy-start(f32[64]{0:T(128)} %param.14) | copy-start | bytes 772
  147.7 40.0 %copy-start.14 = (bf16[1024,256]{1,0:T(8,128)(2,1)S(1)}, bf16[1024,256]{1,0:T(8,128)(2,1)}, u32[]{:S(2)}) copy-start(bf16[1024,256]{1,0:T(8,128)(2,1)} %param.20) | copy-start | bytes 1572868
  147.8 58.6 %all-gather.14.cloned.1.call-start = ((), (), s32[]{:S(2)}) async-start(), calls=%async_computation.4 | async-start | bytes 1310720 | tf_op jit(solution)/shard_map/all_gather | solution.py:118
  147.8 12.9 %collective-permute-start.3 = (bf16[768,256]{1,0:T(8,128)(2,1)S(1)}, bf16[768,256]{1,0:T(8,128)(2,1)S(1)}, u32[]{:S(2)}, u32[]{:S(2)}) collective-permute-start(bf16[768,256]{1,0:T(8,128)(2,1)S(1)} %copy-done.7), channel_id=1, source_target_pairs={{0,12},{4,0},{8,4},{12,8},{1,13},{5,1},{9,5},{13,9},{2,14},{6,2},{... | collective-permute-start | bytes 1179656 | tf_op jit(solution)/shard_map/ppermute | solution.py:30
  151.3 34.0 %collective-permute-start.4 = (bf16[768,256]{1,0:T(8,128)(2,1)S(1)}, bf16[768,256]{1,0:T(8,128)(2,1)S(1)}, u32[]{:S(2)}, u32[]{:S(2)}) collective-permute-start(bf16[768,256]{1,0:T(8,128)(2,1)S(1)} %copy-done.7), channel_id=1, source_target_pairs={{0,8},{4,12},{8,0},{12,4},{1,9},{5,13},{9,1},{13,5},{2,10},{6,14},... | collective-permute-start | bytes 1179656 | tf_op jit(solution)/shard_map/ppermute | solution.py:30
  151.4 34.7 %collective-permute-start.5 = (bf16[768,256]{1,0:T(8,128)(2,1)S(1)}, bf16[768,256]{1,0:T(8,128)(2,1)S(1)}, u32[]{:S(2)}, u32[]{:S(2)}) collective-permute-start(bf16[768,256]{1,0:T(8,128)(2,1)S(1)} %copy-done.7), channel_id=1, source_target_pairs={{0,4},{4,8},{8,12},{12,0},{1,5},{5,9},{9,13},{13,1},{2,6},{6,10},{... | collective-permute-start | bytes 1179656 | tf_op jit(solution)/shard_map/ppermute | solution.py:30
  190.5 72.8 %reduce-scatter.2.cloned.1.call-start = ((), (), s32[]{:S(2)}) async-start(), calls=%async_computation.5 | async-start | bytes 1966080 | tf_op jit(solution)/shard_map/reduce_scatter | solution.py:152
  194.5 11.8 %copy-start.13 = (bf16[2,1024,256]{2,1,0:T(8,128)(2,1)S(1)}, bf16[2,1024,256]{2,1,0:T(8,128)(2,1)}, u32[]{:S(2)}) copy-start(bf16[2,1024,256]{2,1,0:T(8,128)(2,1)} %param.21) | copy-start | bytes 3145732
  205.8 5.4 %copy-start.11 = (f32[256]{0:T(256)S(1)}, f32[256]{0:T(256)}, u32[]{:S(2)}) copy-start(f32[256]{0:T(256)} %param.23) | copy-start | bytes 3076
  209.2 2.0 copy-start.3
  218.1 5.0 %copy-start.8 = (f32[1024]{0:T(1024)}, f32[1024]{0:T(1024)S(1)}, u32[]{:S(2)}) copy-start(f32[1024]{0:T(1024)S(1)} %psum.15) | copy-start | bytes 12292
  218.1 3.6 %copy-start.4 = (f32[2,1024,512]{1,2,0:T(8,128)S(1)}, f32[2,1024,512]{1,2,0:T(8,128)}, u32[]{:S(2)}) copy-start(f32[2,1024,512]{1,2,0:T(8,128)} %copy-done.3) | copy-start | bytes 12582916
  218.3 4.8 %slice-start = ((s8[6291456]{0:T(1024)(128)(4,1)}), s8[4194304]{0:T(1024)(128)(4,1)S(1)}, s32[]{:S(2)}) async-start(s8[6291456]{0:T(1024)(128)(4,1)} %bitcast.123), calls=%async_computation.7 | async-start | bytes 8388608
  221.7 2.0 slice-start.1
  223.1 42.1 %copy-start.1 = (bf16[3,1024,256]{2,1,0:T(8,128)(2,1)S(1)}, bf16[3,1024,256]{2,1,0:T(8,128)(2,1)}, u32[]{:S(2)}) copy-start(bf16[3,1024,256]{2,1,0:T(8,128)(2,1)} %param.19) | copy-start | bytes 4718596
Sparse Core Ops, SparseCore 0:
  9.6 66.2 all-gather.7
  87.8 26.9 all-gather.15
  126.2 14.8 all-gather.9
  147.9 16.7 all-gather.11
  190.6 15.6 all-gather.13
  226.9 36.2 reduce-scatter.1
where the time goes:
time: 273 us; the launch traced here: 272 us
  waiting for transfers between devices  124 us (45%)
  other arithmetic  36.1 us (13%)
  matrix products  33.8 us (12%)
  local copies, waits for them, and re-layouts  31.4 us (12%)
  blocking collectives  25.6 us (9%)
  between operations  14.5 us (5%)
  starting transfers between devices  6.54 us (2%)
    ppermute x6, waiting for transfers between devices, ring_gather(): blocks.append(lax.ppermute(x, axis, [(i, (i - s) % n) for i in range(n)]))  41.8 us
    all_gather x1, waiting for transfers between devices, on_device(): piece = lax.all_gather(kv_weight, 'picks', axis=0, tiled=True)  39.9 us
    reduce_scatter x1, waiting for transfers between devices, on_device(): lax.psum_scatter(jnp.dot(enc.T, dquery, preferred_element_type=jnp.float3...  36.4 us
    another operation x1, other arithmetic  23.6 us
    unnamed x53, local copies, waits for them, and re-layouts  21.8 us
    all_gather x1, blocking collectives, on_device(): lax.all_gather(jnp.stack([top, total]), 'picks', axis=0, tiled=False)  13.3 us
    psum x1, blocking collectives, on_device(): power_two = lax.psum(jnp.sum(latents_out * latents_out, axis=1), 'heads')  6.34 us
    ppermute x6, starting transfers between devices, ring_gather(): blocks.append(lax.ppermute(x, axis, [(i, (i - s) % n) for i in range(n)]))  6.3 us
  transfers between devices with their start and end apart: 12, of which 7 were waited for; matrix products, arithmetic and copies ran while one was open for 24% of the time, Pallas kernels for 0%

commit v1 on v0

--- a/solution.py
+++ b/solution.py
@@ -60,7 +60,26 @@
     column = lax.axis_index("heads") * local
     enc = encode(coords)
     cross_full = ring_gather(cross_out, "heads", n_heads)
-    piece = lax.all_gather(kv_weight, "picks", axis=0, tiled=True)
+    length, place, rows = (lax.axis_size("picks"), lax.axis_index("picks"), kv_weight.shape[0])
+    right = [(i_2, (i_2 + 1) % length) for i_2 in range(length)]
+    behind = [(i_2, (i_2 - 1) % length) for i_2 in range(length)]
+    out_2 = jnp.zeros(
+        (*kv_weight.shape[:0], length * rows, *kv_weight.shape[0 + 1 :]), kv_weight.dtype
+    )
+    out_2 = lax.dynamic_update_slice_in_dim(out_2, kv_weight, place * rows, axis=0)
+    from_left = from_right = kv_weight
+    halfway = length // 2
+    for step in range(1, halfway + 1):
+        from_left = lax.ppermute(from_left, "picks", right)
+        out_2 = lax.dynamic_update_slice_in_dim(
+            out_2, from_left, (place - step) % length * rows, axis=0
+        )
+        if step < length - halfway:
+            from_right = lax.ppermute(from_right, "picks", behind)
+            out_2 = lax.dynamic_update_slice_in_dim(
+                out_2, from_right, (place + step) % length * rows, axis=0
+            )
+    piece = out_2
     keys_vals = jnp.dot(
         enc, piece.reshape(piece.shape[0], 2 * local), preferred_element_type=jnp.float32
     ).astype(jnp.bfloat16)

time: 273 us -> 262 us (0.960)
  waiting for transfers between devices: 124 us -> 97.7 us
  local copies, waits for them, and re-layouts: 31.4 us -> 38.2 us
  starting transfers between devices: 6.54 us -> 12 us
  other arithmetic: 36.1 us -> 39.7 us
    all_gather x1 -> x0, waiting for transfers between devices: 39.9 us -> none  [on_device(): piece = lax.all_gather(kv_weight, 'picks', axis=0, tiled=True)]
    ppermute x0 -> x3, waiting for transfers between devices: none -> 14 us  [the longest x2 14 us: on_device(): from_left = lax.ppermute(from_left, 'picks', right)]
    dynamic_update_slice x0 -> x4, local copies, waits for them, and re-layouts: none -> 5.78 us  [the longest x2 3.45 us: on_device(): lax.dynamic_update_slice_in_dim(out_2, from_left, (place - step) % length...]
    ppermute x0 -> x3, starting transfers between devices: none -> 5.23 us  [the longest x2 3.14 us: on_device(): from_left = lax.ppermute(from_left, 'picks', right)]
    unnamed x53 -> x59, local copies, waits for them, and re-layouts: 21.8 us -> 20.9 us
  transfers between devices with their start and end apart: 12 -> 14, of which waited for: 7 -> 7; matrix products, arithmetic and copies ran while one was open for 24% -> 28% of each run, Pallas kernels for 0% -> 0%
where the time goes in v1:
time: 262 us; the launch traced here: 261 us
  waiting for transfers between devices  97.7 us (37%)
  other arithmetic  39.7 us (15%)
  local copies, waits for them, and re-layouts  38.2 us (15%)
  matrix products  33.6 us (13%)
  blocking collectives  25.3 us (10%)
  between operations  14.3 us (5%)
  starting transfers between devices  12 us (5%)
    ppermute x6, waiting for transfers between devices, ring_gather(): blocks.append(lax.ppermute(x, axis, [(i, (i - s) % n) for i in range(n)]))  40 us
    reduce_scatter x1, waiting for transfers between devices, on_device(): lax.psum_scatter(jnp.dot(enc.T, dquery, preferred_element_type=jnp.float3...  36.4 us
    another operation x1, other arithmetic  25.2 us
    unnamed x59, local copies, waits for them, and re-layouts  20.9 us
    ppermute x2, waiting for transfers between devices, on_device(): from_left = lax.ppermute(from_left, 'picks', right)  14 us
    all_gather x1, blocking collectives, on_device(): lax.all_gather(jnp.stack([top, total]), 'picks', axis=0, tiled=False)  13.3 us
    all_gather x1, waiting for transfers between devices, on_device(): attended_full = lax.all_gather(attended, 'heads', axis=1, tiled=True)  6.73 us
    ppermute x6, starting transfers between devices, ring_gather(): blocks.append(lax.ppermute(x, axis, [(i, (i - s) % n) for i in range(n)]))  6.32 us
  transfers between devices with their start and end apart: 14, of which 7 were waited for; matrix products, arithmetic and copies ran while one was open for 28% of the time, Pallas kernels for 0%

profile of v1, /device:TPU:0, one launch (start us, length us, event | category | flops | bytes accessed | tf_op | source)
XLA Modules:
  0.0 260.8 jit_solution(16369146602328125392)
XLA Ops:
  7.2 3.1 %collective-permute-start = (bf16[768,2,256]{2,1,0:T(2,128)(2,1)}, bf16[768,2,256]{2,1,0:T(2,128)(2,1)}, u32[]{:S(2)}, u32[]{:S(2)}) collective-permute-start(bf16[768,2,256]{2,1,0:T(2,128)(2,1)} %param.16), channel_id=1, source_target_pairs={{0,4},{4,8},{8,12},{12,0},{1,5},{5,9},{9,13},{13,1},{2,6},{6,10},{... | collective-permute-start | bytes 2359304 | tf_op jit(solution)/shard_map/ppermute | solution.py:73
  10.3 2.1 collective-permute-start.1
  12.5 25.2 %fusion = (bf16[3,512,1024]{2,1,0:T(8,128)(2,1)}, bf16[3,512,1024]{2,1,0:T(8,128)(2,1)}) fusion(f32[3,1024]{1,0:T(4,128)} %param.12, f32[512]{0:T(512)S(1)} %maximum_multiply_fusion), kind=kLoop, calls=%fused_computation.2 | loop fusion | flops 4718592 | bytes 6305792 | tf_op jit(solution)/shard_map/convert
  37.9 1.0 constant_dynamic-slice_fusion.3
  39.1 1.7 broadcast_in_dim.4
  41.4 5.1 %pad_maximum_fusion = bf16[6,512,1024]{2,1,0:T(8,128)(2,1)} fusion(bf16[3,512,1024]{2,1,0:T(8,128)(2,1)} %get-tuple-element.19, bf16[3,512,1024]{2,1,0:T(8,128)(2,1)S(1)} %copy-done.5), kind=kLoop, calls=%fused_computation.4 | loop fusion | flops 3145728 | bytes 12582912 | tf_op jit(solution)/shard_map/concatenate | solution.py:18
  46.5 1.7 constant_dynamic-update-slice_fusion.2
  48.2 1.7 constant_dynamic-update-slice_fusion.1
  50.0 14.0 %collective-permute-done.2 = bf16[768,2,256]{2,1,0:T(2,128)(2,1)} collective-permute-done((bf16[768,2,256]{2,1,0:T(2,128)(2,1)}, bf16[768,2,256]{2,1,0:T(2,128)(2,1)}, u32[]{:S(2)}, u32[]{:S(2)}) %collective-permute-start.2) | collective-permute-done | bytes 786464 | tf_op jit(solution)/shard_map/ppermute | solution.py:73
  63.9 1.7 constant_dynamic-update-slice_fusion
  66.2 2.2 copy-done.6
  68.4 3.5 %convolution_convert_fusion.1 = bf16[1024,512]{0,1:T(8,128)(2,1)S(1)} fusion(bf16[3072,1024]{1,0:T(8,128)(2,1)S(1)} %bitcast.123, bf16[3072,512]{1,0:T(8,128)(2,1)S(1)} %bitcast.127), kind=kOutput, calls=%fused_computation.33 | convolution fusion | flops 3221749760 | bytes 10485760 | tf_op jit(solution)/shard_map/dot_general | solution.py:83
  72.1 0.8 multiply_reduce_fusion
  73.0 2.0 copy-done.2
  75.0 1.6 fusion.36
  76.7 1.6 collective-permute-start.4
  79.3 8.7 %collective-permute-done.3 = bf16[256,1024]{1,0:T(8,128)(2,1)S(1)} collective-permute-done((bf16[256,1024]{1,0:T(8,128)(2,1)S(1)}, bf16[256,1024]{1,0:T(8,128)(2,1)S(1)}, u32[]{:S(2)}, u32[]{:S(2)}) %collective-permute-start.3) | collective-permute-done | bytes 524320 | tf_op jit(solution)/shard_map/ppermute | solution.py:30
  88.8 3.1 %fusion.7 = f32[2,512]{1,0:T(2,128)S(1)} fusion(f32[2,512,1024]{2,1,0:T(8,128)} %copy-done.2, f32[2,512]{1,0:T(2,128)S(1)} %get-tuple-element.22), kind=kLoop, calls=%fused_computation.16 | loop fusion | flops 3144704 | bytes 4202496 | tf_op jit(solution)/shard_map/reduce_sum | solution.py:92
  91.9 13.3 %all-gather.1 = f32[8,2,512]{2,1,0:T(2,128)S(1)} all-gather(f32[2,2,512]{2,1,0:T(2,128)S(1)} %pad_maximum_fusion.1), channel_id=3, replica_groups=mesh['groups'=2,'picks'=4,'heads'=4] {'picks'}, dimensions={0}, use_global_device_ids=true | all-gather | bytes 40960 | tf_op jit(solution)/shard_map/all_gather | solution.py:97
  105.2 1.0 copy.81
  106.4 5.3 %fusion.44 = f32[512,2,1,128]{3,2,1,0:T(1,128)S(1)} fusion(f32[4,2,512,1]{0,3,1,2:T(1,128)} %copy.81, bf16[4,2,512,128]{3,2,1,0:T(8,128)(2,1)} %bitcast.156), kind=kOutput, calls=%fused_computation.51 | convolution fusion | flops 6291456 | bytes 1589248 | tf_op jit(solution)/shard_map/phl,phlc->hlc/dot_general | solution.py:101
  113.3 0.8 bitcast_dynamic-update-slice_fusion.2
  114.1 1.9 bitcast_dynamic-update-slice_fusion
  116.0 0.9 bitcast_dynamic-update-slice_fusion.7
  116.9 0.8 bitcast_dynamic-update-slice_fusion.5
  118.5 1.9 bitcast_dynamic-update-slice_fusion.1
  120.4 3.2 %constant_dynamic-slice_fusion.2 = bf16[4,256,1024]{2,1,0:T(8,128)(2,1)} fusion(bf16[8,256,1024]{2,1,0:T(8,128)(2,1)} %bitcast_dynamic-update-slice_fusion.1, s32[]{:T(128)S(6)} %select_n.63), kind=kLoop, calls=%fused_computation.88 | loop fusion | bytes 4194308 | tf_op jit(solution)/shard_map/jit(_roll_dynamic)/dynamic_slice | solution.py:32
  123.7 6.7 %all-gather.7.cloned.1.call-done = bf16[512,1024]{1,0:T(8,128)(2,1)} async-done(((bf16[512,256]{1,0:T(8,128)(2,1)}), bf16[512,1024]{1,0:T(8,128)(2,1)}) %all-gather.7.cloned.1.call-update) | async-done | bytes 1048592 | tf_op jit(solution)/shard_map/all_gather | solution.py:113
  130.4 3.3 %multiply_reduce_fusion.1 = (f32[512]{0:T(512)S(1)}, f32[512,1024]{1,0:T(8,128)S(1)}) fusion(bf16[512,1024]{1,0:T(8,128)(2,1)} %all-gather.7.cloned.1.call-done, bf16[1024,1024]{1,0:T(8,128)(2,1)} %bitcast.128, bf16[512,1024]{1,0:T(8,128)(2,1)S(1)} %copy-done.10), kind=kOutput, calls=%fused_computation.28 | convolution fusion | flops 1075838464 | bytes 6293504 | tf_op jit(solution)/shard_map/dot_general | solution.py:114
  133.7 1.1 fusion.31
  135.6 1.2 convolution_convert_fusion.4
  136.9 3.4 %collective-permute-start.6 = (bf16[768,256]{1,0:T(8,128)(2,1)S(1)}, bf16[768,256]{1,0:T(8,128)(2,1)S(1)}, u32[]{:S(2)}, u32[]{:S(2)}) collective-permute-start(bf16[768,256]{1,0:T(8,128)(2,1)S(1)} %copy-done.8), channel_id=1, source_target_pairs={{0,12},{4,0},{8,4},{12,8},{1,13},{5,1},{9,5},{13,9},{2,14},{6,2},{... | collective-permute-start | bytes 1179656 | tf_op jit(solution)/shard_map/ppermute | solution.py:30
  140.5 1.1 collective-permute-start.8
  142.3 7.5 %collective-permute-done.6 = bf16[768,256]{1,0:T(8,128)(2,1)S(1)} collective-permute-done((bf16[768,256]{1,0:T(8,128)(2,1)S(1)}, bf16[768,256]{1,0:T(8,128)(2,1)S(1)}, u32[]{:S(2)}, u32[]{:S(2)}) %collective-permute-start.6) | collective-permute-done | bytes 393248 | tf_op jit(solution)/shard_map/ppermute | solution.py:30
  150.6 23.8 %collective-permute-done.7 = bf16[768,256]{1,0:T(8,128)(2,1)S(1)} collective-permute-done((bf16[768,256]{1,0:T(8,128)(2,1)S(1)}, bf16[768,256]{1,0:T(8,128)(2,1)S(1)}, u32[]{:S(2)}, u32[]{:S(2)}) %collective-permute-start.7) | collective-permute-done | bytes 393248 | tf_op jit(solution)/shard_map/ppermute | solution.py:30
  176.8 2.7 %multiply_reduce_fusion.2 = (f32[512]{0:T(512)S(1)}, bf16[512,256]{1,0:T(8,128)(2,1)}, f32[512,256]{1,0:T(8,128)}) fusion(f32[256]{0:T(256)S(1)} %bitcast.155, bf16[512,1024]{0,1:T(8,128)(2,1)} %all-gather.9.cloned.1.call-done, bf16[1024,256]{1,0:T(8,128)(2,1)S(1)} %copy-done.17, f32[512,1024]{1,0:T(8,128)} %copy-done.18, s32[]{:T(128)S(6)} %select_n.54), kind=kOutput, calls=%fused_computation.61 | convolution fusion | flops 269090304 | bytes 2886660 | tf_op jit(solution)/shard_map/dot_general | solution.py:135
  182.2 1.5 constant_dynamic-slice_fusion
  183.7 5.0 %convolution_convert_fusion.3 = bf16[1024,256]{0,1:T(8,128)(2,1)S(1)} fusion(bf16[3072,1024]{1,0:T(8,128)(2,1)} %bitcast.122, bf16[3072,256]{1,0:T(8,128)(2,1)S(1)} %bitcast.130), kind=kOutput, calls=%fused_computation.39 | convolution fusion | flops 1610874880 | bytes 8388608 | tf_op jit(solution)/shard_map/dot_general | solution.py:146
  188.7 6.1 %psum.14 = f32[512]{0:T(512)S(1)} all-reduce(f32[512]{0:T(512)S(1)} %get-tuple-element.14), channel_id=1, replica_groups=mesh['groups'=2,'picks'=4,'heads'=4] {'heads'}, use_global_device_ids=true, to_apply=%region_7.8 | all-reduce | flops 512 | bytes 4096 | tf_op jit(solution)/shard_map/psum | solution.py:138
  195.4 2.0 fusion.35
  198.3 2.0 copy-done.3
  200.3 1.0 fusion.32
  201.3 5.9 %psum.15 = f32[1024]{0:T(1024)S(1)} all-reduce(f32[1024]{0:T(1024)S(1)} %fusion.32), channel_id=1, replica_groups=mesh['groups'=2,'picks'=4,'heads'=4] {'heads'}, use_global_device_ids=true, to_apply=%region_10.11 | all-reduce | flops 1024 | bytes 8192 | tf_op jit(solution)/shard_map/psum | solution.py:155
  207.4 3.3 %fusion.2 = f32[2,1024]{1,0:T(2,128)S(1)} fusion(f32[2,512]{1,0:T(2,128)S(1)} %bitcast.149, f32[1024]{0:T(1024)S(1)} %sub.61, f32[2,1024]{1,0:T(2,128)S(1)} %get-tuple-element.29, f32[2,1024,512]{1,2,0:T(8,128)} %copy-done.3), kind=kLoop, calls=%fused_computation.7 | loop fusion | flops 5240832 | bytes 4218880 | tf_op jit(solution)/shard_map/reduce_sum | solution.py:163
  210.8 1.4 fusion.28
  212.8 3.1 %convolution_convert_fusion = bf16[3072,256]{1,0:T(8,128)(2,1)} fusion(bf16[3072,1024]{1,0:T(8,128)(2,1)S(1)} %bitcast.126, bf16[1024,256]{0,1:T(8,128)(2,1)S(1)} %bitcast.157), kind=kOutput, calls=%fused_computation.13 | convolution fusion | flops 1611399168 | bytes 8388608 | tf_op jit(solution)/shard_map/dot_general | solution.py:172
  215.9 36.4 %reduce-scatter.2.cloned.1.call-done = bf16[768,256]{1,0:T(8,128)(2,1)} async-done(((bf16[3072,256]{1,0:T(8,128)(2,1)}), bf16[768,256]{1,0:T(8,128)(2,1)}) %reduce-scatter.2.cloned.1.call-update) | async-done | bytes 393232 | tf_op jit(solution)/shard_map/reduce_scatter | solution.py:171
  252.3 1.9 convert_element_type.100
  (97 shorter events, 15.9 us)
Async XLA Ops:
  7.2 126.5 %copy-start = (bf16[3,1024,256]{2,1,0:T(8,128)(2,1)S(1)}, bf16[3,1024,256]{2,1,0:T(8,128)(2,1)}, u32[]{:S(2)}) copy-start(bf16[3,1024,256]{2,1,0:T(8,128)(2,1)} %param.19) | copy-start | bytes 4718596
  7.2 99.2 %all-gather.13.cloned.1.call-start = ((), (), s32[]{:S(2)}) async-start(), calls=%async_computation.5 | async-start | bytes 1310720 | tf_op jit(solution)/shard_map/all_gather | solution.py:96
  7.2 30.6 %collective-permute-start = (bf16[768,2,256]{2,1,0:T(2,128)(2,1)}, bf16[768,2,256]{2,1,0:T(2,128)(2,1)}, u32[]{:S(2)}, u32[]{:S(2)}) collective-permute-start(bf16[768,2,256]{2,1,0:T(2,128)(2,1)} %param.16), channel_id=1, source_target_pairs={{0,4},{4,8},{8,12},{12,0},{1,5},{5,9},{9,13},{13,1},{2,6},{6,10},{... | collective-permute-start | bytes 2359304 | tf_op jit(solution)/shard_map/ppermute | solution.py:73
  10.3 37.9 %collective-permute-start.1 = (bf16[768,2,256]{2,1,0:T(2,128)(2,1)}, bf16[768,2,256]{2,1,0:T(2,128)(2,1)}, u32[]{:S(2)}, u32[]{:S(2)}) collective-permute-start(bf16[768,2,256]{2,1,0:T(2,128)(2,1)} %param.16), channel_id=1, source_target_pairs={{0,12},{4,0},{8,4},{12,8},{1,13},{5,1},{9,5},{13,9},{2,14},{6,2},{... | collective-permute-start | bytes 2359304 | tf_op jit(solution)/shard_map/ppermute | solution.py:78
  37.7 3.1 %copy-start.9 = (bf16[768,2,256]{2,1,0:T(2,128)(2,1)S(1)}, bf16[768,2,256]{2,1,0:T(2,128)(2,1)}, u32[]{:S(2)}) copy-start(bf16[768,2,256]{2,1,0:T(2,128)(2,1)} %param.16) | copy-start | bytes 2359300
  37.8 26.1 %collective-permute-start.2 = (bf16[768,2,256]{2,1,0:T(2,128)(2,1)}, bf16[768,2,256]{2,1,0:T(2,128)(2,1)}, u32[]{:S(2)}, u32[]{:S(2)}) collective-permute-start(bf16[768,2,256]{2,1,0:T(2,128)(2,1)} %collective-permute-done), channel_id=1, source_target_pairs={{0,4},{4,8},{8,12},{12,0},{1,5},{5,9},{9,13},{13,1},{2,6},{6,10},{... | collective-permute-start | bytes 2359304 | tf_op jit(solution)/shard_map/ppermute | solution.py:73
  39.1 2.3 copy-start.5
  65.7 2.8 %copy-start.6 = (bf16[6,512,1024]{2,1,0:T(8,128)(2,1)S(1)}, bf16[6,512,1024]{2,1,0:T(8,128)(2,1)}, u32[]{:S(2)}) copy-start(bf16[6,512,1024]{2,1,0:T(8,128)(2,1)} %pad_maximum_fusion) | copy-start | bytes 18874372
  72.9 2.0 copy-start.2
  72.9 3.7 %copy-start.7 = (bf16[256,1024]{1,0:T(8,128)(2,1)S(1)}, bf16[256,1024]{1,0:T(8,128)(2,1)}, u32[]{:S(2)}) copy-start(bf16[256,1024]{1,0:T(8,128)(2,1)} %param.17) | copy-start | bytes 1572868
  72.9 5.5 %copy-start.12 = (f32[2,1024]{1,0:T(2,128)S(1)}, f32[2,1024]{1,0:T(2,128)}, u32[]{:S(2)}) copy-start(f32[2,1024]{1,0:T(2,128)} %param.18) | copy-start | bytes 24580
  76.6 53.8 %all-gather.7.cloned.1.call-start = ((), (), s32[]{:S(2)}) async-start(), calls=%async_computation.1 | async-start | bytes 1310720 | tf_op jit(solution)/shard_map/all_gather | solution.py:113
  76.6 11.3 %collective-permute-start.3 = (bf16[256,1024]{1,0:T(8,128)(2,1)S(1)}, bf16[256,1024]{1,0:T(8,128)(2,1)S(1)}, u32[]{:S(2)}, u32[]{:S(2)}) collective-permute-start(bf16[256,1024]{1,0:T(8,128)(2,1)S(1)} %copy-done.7), channel_id=1, source_target_pairs={{0,3},{1,0},{2,1},{3,2},{4,7},{5,4},{6,5},{7,6},{8,11},{9,8},{10,9... | collective-permute-start | bytes 1572872 | tf_op jit(solution)/shard_map/ppermute | solution.py:30
  76.7 36.6 %collective-permute-start.4 = (bf16[256,1024]{1,0:T(8,128)(2,1)S(1)}, bf16[256,1024]{1,0:T(8,128)(2,1)S(1)}, u32[]{:S(2)}, u32[]{:S(2)}) collective-permute-start(bf16[256,1024]{1,0:T(8,128)(2,1)S(1)} %copy-done.7), channel_id=1, source_target_pairs={{0,2},{1,3},{2,0},{3,1},{4,6},{5,7},{6,4},{7,5},{8,10},{9,11},{10,... | collective-permute-start | bytes 1572872 | tf_op jit(solution)/shard_map/ppermute | solution.py:30
  78.2 35.9 %collective-permute-start.5 = (bf16[256,1024]{1,0:T(8,128)(2,1)S(1)}, bf16[256,1024]{1,0:T(8,128)(2,1)}, u32[]{:S(2)}, u32[]{:S(2)}) collective-permute-start(bf16[256,1024]{1,0:T(8,128)(2,1)S(1)} %copy-done.7), channel_id=1, source_target_pairs={{0,1},{1,2},{2,3},{3,0},{4,5},{5,6},{6,7},{7,4},{8,9},{9,10},{10,1... | collective-permute-start | bytes 1572872 | tf_op jit(solution)/shard_map/ppermute | solution.py:30
  113.2 63.6 %all-gather.9.cloned.1.call-start = ((), (), s32[]{:S(2)}) async-start(), calls=%async_computation.2 | async-start | bytes 1310720 | tf_op jit(solution)/shard_map/all_gather | solution.py:134
  117.7 12.7 %copy-start.10 = (bf16[512,1024]{1,0:T(8,128)(2,1)S(1)}, bf16[512,1024]{1,0:T(8,128)(2,1)}, u32[]{:S(2)}) copy-start(bf16[512,1024]{1,0:T(8,128)(2,1)} %param.15) | copy-start | bytes 3145732
  133.7 1.3 copy-start.18
  135.5 1.4 copy-start.8
  135.5 4.7 %copy-start.13 = (s32[1024]{0:T(1024)S(1)}, s32[1024]{0:T(1024)}, u32[]{:S(2)}) copy-start(s32[1024]{0:T(1024)} %param.13) | copy-start | bytes 12292
  135.5 4.7 %copy-start.15 = (f32[64]{0:T(128)S(1)}, f32[64]{0:T(128)}, u32[]{:S(2)}) copy-start(f32[64]{0:T(128)} %param.14) | copy-start | bytes 772
  136.8 40.0 %copy-start.17 = (bf16[1024,256]{1,0:T(8,128)(2,1)S(1)}, bf16[1024,256]{1,0:T(8,128)(2,1)}, u32[]{:S(2)}) copy-start(bf16[1024,256]{1,0:T(8,128)(2,1)} %param.20) | copy-start | bytes 1572868
  136.8 58.6 %all-gather.11.cloned.1.call-start = ((), (), s32[]{:S(2)}) async-start(), calls=%async_computation.3 | async-start | bytes 1310720 | tf_op jit(solution)/shard_map/all_gather | solution.py:137
  136.9 12.9 %collective-permute-start.6 = (bf16[768,256]{1,0:T(8,128)(2,1)S(1)}, bf16[768,256]{1,0:T(8,128)(2,1)S(1)}, u32[]{:S(2)}, u32[]{:S(2)}) collective-permute-start(bf16[768,256]{1,0:T(8,128)(2,1)S(1)} %copy-done.8), channel_id=1, source_target_pairs={{0,12},{4,0},{8,4},{12,8},{1,13},{5,1},{9,5},{13,9},{2,14},{6,2},{... | collective-permute-start | bytes 1179656 | tf_op jit(solution)/shard_map/ppermute | solution.py:30
  140.4 34.0 %collective-permute-start.7 = (bf16[768,256]{1,0:T(8,128)(2,1)S(1)}, bf16[768,256]{1,0:T(8,128)(2,1)S(1)}, u32[]{:S(2)}, u32[]{:S(2)}) collective-permute-start(bf16[768,256]{1,0:T(8,128)(2,1)S(1)} %copy-done.8), channel_id=1, source_target_pairs={{0,8},{4,12},{8,0},{12,4},{1,9},{5,13},{9,1},{13,5},{2,10},{6,14},... | collective-permute-start | bytes 1179656 | tf_op jit(solution)/shard_map/ppermute | solution.py:30
  140.5 34.7 %collective-permute-start.8 = (bf16[768,256]{1,0:T(8,128)(2,1)S(1)}, bf16[768,256]{1,0:T(8,128)(2,1)S(1)}, u32[]{:S(2)}, u32[]{:S(2)}) collective-permute-start(bf16[768,256]{1,0:T(8,128)(2,1)S(1)} %copy-done.8), channel_id=1, source_target_pairs={{0,4},{4,8},{8,12},{12,0},{1,5},{5,9},{9,13},{13,1},{2,6},{6,10},{... | collective-permute-start | bytes 1179656 | tf_op jit(solution)/shard_map/ppermute | solution.py:30
  179.5 72.8 %reduce-scatter.2.cloned.1.call-start = ((), (), s32[]{:S(2)}) async-start(), calls=%async_computation.4 | async-start | bytes 1966080 | tf_op jit(solution)/shard_map/reduce_scatter | solution.py:171
  183.7 11.7 %copy-start.16 = (bf16[2,1024,256]{2,1,0:T(8,128)(2,1)S(1)}, bf16[2,1024,256]{2,1,0:T(8,128)(2,1)}, u32[]{:S(2)}) copy-start(bf16[2,1024,256]{2,1,0:T(8,128)(2,1)} %param.21) | copy-start | bytes 3145732
  197.4 2.9 %copy-start.14 = (f32[256]{0:T(256)S(1)}, f32[256]{0:T(256)}, u32[]{:S(2)}) copy-start(f32[256]{0:T(256)} %param.23) | copy-start | bytes 3076
  198.3 2.0 copy-start.3
  207.2 5.0 %copy-start.11 = (f32[1024]{0:T(1024)}, f32[1024]{0:T(1024)S(1)}, u32[]{:S(2)}) copy-start(f32[1024]{0:T(1024)S(1)} %psum.15) | copy-start | bytes 12292
  207.2 3.6 %copy-start.4 = (f32[2,1024,512]{1,2,0:T(8,128)S(1)}, f32[2,1024,512]{1,2,0:T(8,128)}, u32[]{:S(2)}) copy-start(f32[2,1024,512]{1,2,0:T(8,128)} %copy-done.3) | copy-start | bytes 12582916
  207.4 4.8 %slice-start = ((s8[6291456]{0:T(1024)(128)(4,1)}), s8[4194304]{0:T(1024)(128)(4,1)S(1)}, s32[]{:S(2)}) async-start(s8[6291456]{0:T(1024)(128)(4,1)} %bitcast.124), calls=%async_computation.6 | async-start | bytes 8388608
  210.8 2.0 slice-start.1
  212.7 41.5 %copy-start.1 = (bf16[3,1024,256]{2,1,0:T(8,128)(2,1)S(1)}, bf16[3,1024,256]{2,1,0:T(8,128)(2,1)}, u32[]{:S(2)}) copy-start(bf16[3,1024,256]{2,1,0:T(8,128)(2,1)} %param.19) | copy-start | bytes 4718596
Sparse Core Ops, SparseCore 0:
  76.7 27.7 all-gather.12
  113.3 17.0 all-gather.6
  136.9 16.7 all-gather.8
  179.6 15.7 all-gather.10
  216.0 36.2 reduce-scatter.1
